TPU v7x, 256 devices: a whole 4x4x8 slice. The times are simulated.
256 devices in a mesh: dp: 16 (over x, y_hi, core), mp: 16 (over y_lo, z).
Axes of the slice: x: 4, y: 4 (y_hi: 2, y_lo: 2; y = y_hi * 2 + y_lo), z: 8, core: 2. Of those that a mesh axis runs over, the one named last changes fastest.
Arguments:
- tokens: bfloat16 [4096, 4096], P('dp'), may hold values from -32 to 32
- weights: bfloat16 [4096, 2, 3, 4096], P('dp', None, None, 'mp'), may hold values from -1 to 1
- block_modality: int32 [32], replicated, may hold values from 0 to 1
- doc_ids: int32 [4096], replicated, may hold values from 0 to 31, never falling along the last dimension, each value on 1 to 1024 neighbouring positions
- grad_out: bfloat16 [4096, 4096], P('dp', 'mp'), may hold values from -6 to 6
Outputs:
- attended: bfloat16 [4096, 4096], P('dp', 'mp')
- grad_tokens: bfloat16 [4096, 4096], P('dp', 'mp')
- grad_weights: bfloat16 [4096, 2, 3, 4096], P('dp', None, None, 'mp')
Inputs may be any that keep to these rules, and one draw needn't show every extreme that they name: doc_ids never falls along the sequence; a document is a run of equal ids of at most 1024 tokens, and one document has exactly 1024.
All inputs are finite; a program needn't handle non-finite values.
Results may differ from a plain program's by a relative error of at most 0.025.
Values may be sent and summed in bfloat16 or wider, within the bound.
No kernel may reach another device: no remote copies, remote signals or barrier semaphores. Data moves between devices by JAX's collectives and lax.ppermute only.
A program may use at most 128 MiB of HBM per device.

v0:
```python
import jax
import jax.numpy as jnp
from jax import lax
from jax.sharding import PartitionSpec as P

HD = 128
BLOCK = 128
SPAN = 4


def shifted(block, axis, distance):
    devices = range(lax.axis_size(axis))
    route = [(i - distance, i) for i in devices if i - distance in devices]
    return lax.ppermute(block, axis, route)


def split_by_modality(rows, is_image):
    zeros = jnp.zeros_like(rows)
    text = jnp.where(is_image[:, None], zeros, rows)
    image = jnp.where(is_image[:, None], rows, zeros)
    return jnp.stack([text, image], axis=2).reshape(rows.shape[0], 2 * rows.shape[1])


def split_by_modality_major(rows, is_image):
    zeros = jnp.zeros_like(rows)
    text = jnp.where(is_image[:, None], zeros, rows)
    image = jnp.where(is_image[:, None], rows, zeros)
    return jnp.concatenate([text, image], axis=1)


def on_device(tokens, weights, block_modality, doc_ids, grad_out):
    local_rows = tokens.shape[0]
    width_rows = weights.shape[0]
    head_width = weights.shape[3]
    head_count = head_width // HD
    dp_devices = lax.axis_size("dp")
    mp_devices = lax.axis_size("mp")
    local_blocks = local_rows // BLOCK
    front_pad = SPAN * local_rows
    window_len = front_pad + local_rows
    my_index = lax.axis_index("dp")
    scale_factor = HD ** (-0.5)
    token_image = jnp.repeat(block_modality, BLOCK) == 1
    my_image = lax.dynamic_slice_in_dim(token_image, my_index * local_rows, local_rows, 0)
    flat_weights = weights.reshape(width_rows, 2, 3 * head_width)
    whole_weights = lax.all_gather(flat_weights, "dp", axis=0, tiled=True)
    columns = lax.all_to_all(tokens, "dp", split_axis=1, concat_axis=0, tiled=True)
    whole_weights, columns = lax.optimization_barrier((whole_weights, columns))
    stacked_weights = whole_weights.reshape(-1, 3 * head_width)
    summed = jnp.dot(
        split_by_modality(tokens, my_image), stacked_weights, preferred_element_type=jnp.float32
    )
    qkv = summed.astype(jnp.bfloat16).reshape(local_rows, 3, head_count, HD)
    queries = qkv[:, 0]
    key_values = qkv[:, 1:]
    received = []
    for distance in range(SPAN, 0, -1):
        received.append(shifted(key_values, "dp", distance))
    window = jnp.concatenate(received + [key_values], 0)
    key_rows = window[:, 0]
    value_rows = window[:, 1]
    docs_pad = jnp.concatenate([jnp.full((front_pad,), -1, jnp.int32), doc_ids], 0)
    key_docs = lax.dynamic_slice_in_dim(docs_pad, my_index * local_rows, window_len, 0)
    query_docs = lax.dynamic_slice_in_dim(doc_ids, my_index * local_rows, local_rows, 0)
    offsets = jnp.arange(window_len, dtype=jnp.int32) - front_pad
    allowed = (key_docs[None, :] == query_docs[:, None]) & (
        offsets[None, :] <= jnp.arange(local_rows, dtype=jnp.int32)[:, None]
    )
    scores = (
        jnp.einsum("qhd,khd->hqk", queries, key_rows, preferred_element_type=jnp.float32)
        * scale_factor
    )
    scores = jnp.where(allowed[None], scores, -1e30)
    top_score = jnp.max(scores, axis=-1, keepdims=True)
    expos = jnp.where(allowed[None], jnp.exp(scores - top_score), 0.0)
    probs_f = expos / jnp.sum(expos, axis=-1, keepdims=True)
    probs = probs_f.astype(jnp.bfloat16)
    attended = jnp.einsum("hqk,khd->qhd", probs, value_rows, preferred_element_type=jnp.float32)
    attended = attended.astype(jnp.bfloat16).reshape(local_rows, head_width)
    upstream = grad_out.reshape(local_rows, head_count, HD)
    dprob = jnp.einsum("qhd,khd->hqk", upstream, value_rows, preferred_element_type=jnp.float32)
    row_delta = jnp.sum(probs_f * dprob, axis=-1, keepdims=True)
    dscore = (probs_f * (dprob - row_delta)).astype(jnp.bfloat16)
    grad_q = (
        jnp.einsum("hqk,khd->qhd", dscore, key_rows, preferred_element_type=jnp.float32)
        * scale_factor
    )
    grad_k = (
        jnp.einsum("hqk,qhd->khd", dscore, queries, preferred_element_type=jnp.float32)
        * scale_factor
    )
    grad_v = jnp.einsum("hqk,qhd->khd", probs, upstream, preferred_element_type=jnp.float32)
    window_grads = jnp.stack([grad_k, grad_v], 1)
    own_grads = window_grads[front_pad:]
    for distance in range(1, SPAN + 1):
        lower_edge = front_pad - distance * local_rows
        sent_block = window_grads[lower_edge : lower_edge + local_rows]
        own_grads = own_grads + shifted(sent_block.astype(jnp.bfloat16), "dp", -distance).astype(
            sent_block.dtype
        )
    dqkv = (
        jnp.concatenate([grad_q[:, None], own_grads], 1)
        .astype(jnp.bfloat16)
        .reshape(local_rows, 3 * head_width)
    )
    parts = lax.dot_general(
        split_by_modality_major(dqkv, my_image),
        whole_weights.reshape(whole_weights.shape[0], -1),
        (((1,), (1,)), ((), ())),
        preferred_element_type=jnp.float32,
    ).astype(jnp.bfloat16)
    group_parts = lax.all_to_all(
        parts.reshape(local_rows, mp_devices, -1), "mp", split_axis=1, concat_axis=1, tiled=True
    )
    grad_tokens = jnp.sum(group_parts.astype(jnp.float32), axis=1).astype(jnp.bfloat16)
    gathered = lax.all_gather(dqkv, "dp", axis=0, tiled=True)
    weight_sum = lax.dot_general(
        columns,
        split_by_modality_major(gathered, token_image),
        (((0,), (0,)), ((), ())),
        preferred_element_type=jnp.float32,
    )
    grad_weights = weight_sum.astype(jnp.bfloat16).reshape(width_rows, 2, 3, head_width)
    return (attended, grad_tokens, grad_weights)


def solution(mesh):
    return jax.shard_map(
        on_device,
        mesh=mesh,
        in_specs=(P("dp", None), P("dp", None, None, "mp"), P(), P(), P("dp", "mp")),
        out_specs=(P("dp", "mp"), P("dp", "mp"), P("dp", None, None, "mp")),
        check_vma=False,
    )
```

profile of v0, /device:TPU:33, one launch (start us, length us, event | category | flops | bytes accessed | tf_op | source)
XLA Modules:
  0.0 316.9 jit_solution(15968421403756851934)
XLA Ops:
  7.2 3.2 copy.46
  10.4 2.5 copy.47
  12.9 7.7 %all-to-all-start = ((bf16[256,16,256]{0,2,1:T(8,128)(2,1)}), bf16[256,16,256]{0,2,1:T(8,128)(2,1)}, u32[]{:S(2)}, u32[]{:S(2)}) async-start(bf16[256,16,256]{0,2,1:T(8,128)(2,1)} %bitcast.76), calls=%async_computation | async-start | bytes 4194304 | tf_op jit(solution)/shard_map/all_to_all | solution.py:47
  21.0 2.3 select_bitcast_fusion.1
  23.3 33.3 %all-to-all-done = bf16[256,16,256]{0,2,1:T(8,128)(2,1)} async-done(((bf16[256,16,256]{0,2,1:T(8,128)(2,1)}), bf16[256,16,256]{0,2,1:T(8,128)(2,1)}, u32[]{:S(2)}, u32[]{:S(2)}) %all-to-all-start) | async-done | bytes 2097184 | tf_op jit(solution)/shard_map/all_to_all | solution.py:47
  56.6 4.1 %copy.48 = bf16[16,256,256]{2,1,0:T(8,128)(2,1)} copy(bf16[16,256,256]{1,2,0:T(8,128)(2,1)} %bitcast.5) | data formatting | bytes 4194304 | tf_op jit(solution)/shard_map/all_to_all | solution.py:47
  60.7 75.9 %all-gather.3.cloned.1.call-done = bf16[4096,2,768]{0,2,1:T(8,128)(2,1)} async-done(((bf16[256,2,768]{0,2,1:T(8,128)(2,1)}), bf16[4096,2,768]{0,2,1:T(8,128)(2,1)}) %all-gather.3.cloned.1.call-update) | async-done | bytes 12582928 | tf_op jit(solution)/shard_map/all_gather | solution.py:46
  136.6 8.6 %fusion.22 = bf16[256,768]{1,0:T(8,128)(2,1)S(1)} fusion(bf16[4096,2,768]{0,2,1:T(8,128)(2,1)} %all-gather.3.cloned.1.call-done, bf16[256,4096,1]{1,0,2:T(8,128)(2,1)} %get-tuple-element.22, bf16[256,4096,1]{1,0,2:T(8,128)(2,1)S(1)} %copy-done.2), kind=kOutput, calls=%fused_computation.35 | convolution fusion | flops 3223519232 | bytes 17170432 | tf_op jit(solution)/shard_map/dot_general | solution.py:50
  145.6 2.8 collective-permute-start
  150.5 2.1 collective-permute-start.2
  153.0 5.0 %collective-permute-start.3 = (bf16[256,2,2,128]{3,0,2,1:T(8,128)(2,1)S(1)}, bf16[256,2,2,128]{3,0,2,1:T(8,128)(2,1)S(1)}, u32[]{:S(2)}, u32[]{:S(2)}) collective-permute-start(bf16[256,2,2,128]{3,0,2,1:T(8,128)(2,1)S(1)} %copy.67), channel_id=1, source_target_pairs={{0,16},{16,32},{32,48},{48,64},{64,80},{80,96},{96,112},{112,128},... | collective-permute-start | bytes 786440 | tf_op jit(solution)/shard_map/ppermute | solution.py:14
  160.4 2.4 collective-permute-done.3
  164.4 2.5 fusion.45
  166.9 2.2 multiply_reduce_fusion
  174.6 2.1 collective-permute-start.4
  178.3 3.4 %collective-permute-done.7 = bf16[256,2,2,128]{0,3,2,1:T(8,128)(2,1)S(1)} collective-permute-done((bf16[256,2,2,128]{0,3,2,1:T(8,128)(2,1)S(1)}, bf16[256,2,2,128]{0,3,2,1:T(8,128)(2,1)S(1)}, u32[]{:S(2)}, u32[]{:S(2)}) %collective-permute-start.7) | collective-permute-done | bytes 262176 | tf_op jit(solution)/shard_map/ppermute | solution.py:14
  181.7 10.9 %collective-permute-done.6 = bf16[256,2,2,128]{0,3,2,1:T(8,128)(2,1)S(1)} collective-permute-done((bf16[256,2,2,128]{0,3,2,1:T(8,128)(2,1)S(1)}, bf16[256,2,2,128]{0,3,2,1:T(8,128)(2,1)S(1)}, u32[]{:S(2)}, u32[]{:S(2)}) %collective-permute-start.6) | collective-permute-done | bytes 262176 | tf_op jit(solution)/shard_map/ppermute | solution.py:14
  194.7 8.3 %convolution_convert_fusion = bf16[256,4096]{1,0:T(8,128)(2,1)S(1)} fusion(bf16[4096,1536]{0,1:T(8,128)(2,1)} %bitcast.74, bf16[256,768]{0,1:T(8,128)(2,1)S(1)} %get-tuple-element.28, bf16[256,768]{0,1:T(8,128)(2,1)S(1)} %get-tuple-element.27), kind=kOutput, calls=%fused_computation.7 | convolution fusion | flops 3223846912 | bytes 15466496 | tf_op jit(solution)/shard_map/dot_general | solution.py:106
  204.6 7.9 %all-to-all-start.1 = ((bf16[256,16,256]{2,0,1:T(8,128)(2,1)}), bf16[256,16,256]{2,0,1:T(8,128)(2,1)S(1)}, u32[]{:S(2)}, u32[]{:S(2)}) async-start(bf16[256,16,256]{2,0,1:T(8,128)(2,1)} %bitcast.77), calls=%async_computation.1 | async-start | bytes 4194304 | tf_op jit(solution)/shard_map/all_to_all | solution.py:112
  212.5 2.7 convolution_convert_fusion.1
  216.0 42.3 %all-to-all-done.1 = bf16[256,16,256]{2,0,1:T(8,128)(2,1)S(1)} async-done(((bf16[256,16,256]{2,0,1:T(8,128)(2,1)}), bf16[256,16,256]{2,0,1:T(8,128)(2,1)S(1)}, u32[]{:S(2)}, u32[]{:S(2)}) %all-to-all-start.1) | async-done | bytes 2097184 | tf_op jit(solution)/shard_map/all_to_all | solution.py:112
  259.2 31.4 %all-gather.5.cloned.1.call-done = bf16[4096,768]{0,1:T(8,128)(2,1)} async-done(((bf16[256,768]{0,1:T(8,128)(2,1)}), bf16[4096,768]{0,1:T(8,128)(2,1)}) %all-gather.5.cloned.1.call-update) | async-done | bytes 6291472 | tf_op jit(solution)/shard_map/all_gather | solution.py:116
  290.7 6.3 %broadcast_select_fusion.1 = (bf16[4096,768]{0,1:T(8,128)(2,1)S(1)}, bf16[4096,768]{0,1:T(8,128)(2,1)}) fusion(bf16[4096,768]{0,1:T(8,128)(2,1)} %all-gather.5.cloned.1.call-done, pred[4096]{0:T(1024)(128)(4,1)S(1)} %broadcast_bitcast_fusion), kind=kLoop, calls=%fused_computation.6 | loop fusion | flops 6291456 | bytes 18878464 | tf_op jit(solution)/shard_map/jit(_where)/select_n | solution.py:26
  297.0 9.9 %fusion.15 = bf16[256,1536]{1,0:T(8,128)(2,1)} fusion(bf16[4096,256]{1,0:T(8,128)(2,1)} %bitcast.81, bf16[4096,768]{0,1:T(8,128)(2,1)} %get-tuple-element.20, bf16[4096,768]{0,1:T(8,128)(2,1)S(1)} %get-tuple-element.19), kind=kOutput, calls=%fused_computation.27 | convolution fusion | flops 3246784512 | bytes 15466496 | tf_op jit(solution)/shard_map/dot_general | solution.py:117
  (55 shorter events, 22.6 us)
Async XLA Ops:
  7.2 3.2 %copy-start = (bf16[256,4096]{1,0:T(8,128)(2,1)S(1)}, bf16[256,4096]{1,0:T(8,128)(2,1)}, u32[]{:S(2)}) copy-start(bf16[256,4096]{1,0:T(8,128)(2,1)} %param.5) | copy-start | bytes 6291460
  7.2 129.4 %all-gather.3.cloned.1.call-start = ((), (), s32[]{:S(2)}) async-start(), calls=%async_computation.2 | async-start | bytes 13369344 | tf_op jit(solution)/shard_map/all_gather | solution.py:46
  12.9 7.8 %copy-start.5 = (s32[32]{0:T(128)S(1)}, s32[32]{0:T(128)}, u32[]{:S(2)}) copy-start(s32[32]{0:T(128)} %param.7) | copy-start | bytes 388
  12.9 8.0 %copy-start.4 = (s32[4096]{0:T(1024)S(1)}, s32[4096]{0:T(1024)}, u32[]{:S(2)}) copy-start(s32[4096]{0:T(1024)} %param.8) | copy-start | bytes 49156
  12.9 43.7 %all-to-all-start = ((bf16[256,16,256]{0,2,1:T(8,128)(2,1)}), bf16[256,16,256]{0,2,1:T(8,128)(2,1)}, u32[]{:S(2)}, u32[]{:S(2)}) async-start(bf16[256,16,256]{0,2,1:T(8,128)(2,1)} %bitcast.76), calls=%async_computation | async-start | bytes 4194304 | tf_op jit(solution)/shard_map/all_to_all | solution.py:47
  20.6 270.1 %all-gather.5.cloned.1.call-start = ((), (), s32[]{:S(2)}) async-start(), calls=%async_computation.3 | async-start | bytes 6684672 | tf_op jit(solution)/shard_map/all_gather | solution.py:116
  56.6 80.0 %copy-start.2 = (bf16[256,4096,1]{1,0,2:T(8,128)(2,1)S(1)}, bf16[256,4096,1]{1,0,2:T(8,128)(2,1)}, u32[]{:S(2)}) copy-start(bf16[256,4096,1]{1,0,2:T(8,128)(2,1)} %get-tuple-element.21) | copy-start | bytes 6291460
  145.2 7.7 %copy-start.3 = (bf16[256,256]{1,0:T(8,128)(2,1)S(1)}, bf16[256,256]{1,0:T(8,128)(2,1)}, u32[]{:S(2)}) copy-start(bf16[256,256]{1,0:T(8,128)(2,1)} %param.9) | copy-start | bytes 393220
  145.6 12.6 %collective-permute-start = (bf16[256,2,2,128]{3,0,2,1:T(8,128)(2,1)S(1)}, bf16[256,2,2,128]{3,0,2,1:T(8,128)(2,1)S(1)}, u32[]{:S(2)}, u32[]{:S(2)}) collective-permute-start(bf16[256,2,2,128]{3,0,2,1:T(8,128)(2,1)S(1)} %copy.67), channel_id=1, source_target_pairs={{0,64},{16,80},{32,96},{48,112},{64,128},{80,144},{96,160},{112,17... | collective-permute-start | bytes 786440 | tf_op jit(solution)/shard_map/ppermute | solution.py:14
  148.4 10.5 %collective-permute-start.1 = (bf16[256,2,2,128]{3,0,2,1:T(8,128)(2,1)S(1)}, bf16[256,2,2,128]{3,0,2,1:T(8,128)(2,1)S(1)}, u32[]{:S(2)}, u32[]{:S(2)}) collective-permute-start(bf16[256,2,2,128]{3,0,2,1:T(8,128)(2,1)S(1)} %copy.67), channel_id=1, source_target_pairs={{0,48},{16,64},{32,80},{48,96},{64,112},{80,128},{96,144},{112,160... | collective-permute-start | bytes 786440 | tf_op jit(solution)/shard_map/ppermute | solution.py:14
  150.5 9.2 %collective-permute-start.2 = (bf16[256,2,2,128]{3,0,2,1:T(8,128)(2,1)S(1)}, bf16[256,2,2,128]{3,0,2,1:T(8,128)(2,1)S(1)}, u32[]{:S(2)}, u32[]{:S(2)}) collective-permute-start(bf16[256,2,2,128]{3,0,2,1:T(8,128)(2,1)S(1)} %copy.67), channel_id=1, source_target_pairs={{0,32},{16,48},{32,64},{48,80},{64,96},{80,112},{96,128},{112,144}... | collective-permute-start | bytes 786440 | tf_op jit(solution)/shard_map/ppermute | solution.py:14
  153.0 9.8 %collective-permute-start.3 = (bf16[256,2,2,128]{3,0,2,1:T(8,128)(2,1)S(1)}, bf16[256,2,2,128]{3,0,2,1:T(8,128)(2,1)S(1)}, u32[]{:S(2)}, u32[]{:S(2)}) collective-permute-start(bf16[256,2,2,128]{3,0,2,1:T(8,128)(2,1)S(1)} %copy.67), channel_id=1, source_target_pairs={{0,16},{16,32},{32,48},{48,64},{64,80},{80,96},{96,112},{112,128},... | collective-permute-start | bytes 786440 | tf_op jit(solution)/shard_map/ppermute | solution.py:14
  166.9 2.6 copy-start.1
  170.7 11.1 %collective-permute-start.7 = (bf16[256,2,2,128]{0,3,2,1:T(8,128)(2,1)S(1)}, bf16[256,2,2,128]{0,3,2,1:T(8,128)(2,1)S(1)}, u32[]{:S(2)}, u32[]{:S(2)}) collective-permute-start(bf16[256,2,2,128]{0,3,2,1:T(8,128)(2,1)S(1)} %get-tuple-element.24), channel_id=1, source_target_pairs={{64,0},{80,16},{96,32},{112,48},{128,64},{144,80},{160,96},{176,11... | collective-permute-start | bytes 786440 | tf_op jit(solution)/shard_map/ppermute | solution.py:14
  172.0 20.7 %collective-permute-start.6 = (bf16[256,2,2,128]{0,3,2,1:T(8,128)(2,1)S(1)}, bf16[256,2,2,128]{0,3,2,1:T(8,128)(2,1)S(1)}, u32[]{:S(2)}, u32[]{:S(2)}) collective-permute-start(bf16[256,2,2,128]{0,3,2,1:T(8,128)(2,1)S(1)} %get-tuple-element.25), channel_id=1, source_target_pairs={{48,0},{64,16},{80,32},{96,48},{112,64},{128,80},{144,96},{160,112... | collective-permute-start | bytes 786440 | tf_op jit(solution)/shard_map/ppermute | solution.py:14
  173.3 19.4 %collective-permute-start.5 = (bf16[256,2,2,128]{0,3,2,1:T(8,128)(2,1)S(1)}, bf16[256,2,2,128]{0,3,2,1:T(8,128)(2,1)S(1)}, u32[]{:S(2)}, u32[]{:S(2)}) collective-permute-start(bf16[256,2,2,128]{0,3,2,1:T(8,128)(2,1)S(1)} %get-tuple-element.26), channel_id=1, source_target_pairs={{32,0},{48,16},{64,32},{80,48},{96,64},{112,80},{128,96},{144,112}... | collective-permute-start | bytes 786440 | tf_op jit(solution)/shard_map/ppermute | solution.py:14
  174.6 18.1 %collective-permute-start.4 = (bf16[256,2,2,128]{0,3,2,1:T(8,128)(2,1)S(1)}, bf16[256,2,2,128]{0,3,2,1:T(8,128)(2,1)S(1)}, u32[]{:S(2)}, u32[]{:S(2)}) collective-permute-start(bf16[256,2,2,128]{0,3,2,1:T(8,128)(2,1)S(1)} %get-tuple-element.23), channel_id=1, source_target_pairs={{16,0},{32,16},{48,32},{64,48},{80,64},{96,80},{112,96},{128,112},... | collective-permute-start | bytes 786440 | tf_op jit(solution)/shard_map/ppermute | solution.py:14
  204.6 53.7 %all-to-all-start.1 = ((bf16[256,16,256]{2,0,1:T(8,128)(2,1)}), bf16[256,16,256]{2,0,1:T(8,128)(2,1)S(1)}, u32[]{:S(2)}, u32[]{:S(2)}) async-start(bf16[256,16,256]{2,0,1:T(8,128)(2,1)} %bitcast.77), calls=%async_computation.1 | async-start | bytes 4194304 | tf_op jit(solution)/shard_map/all_to_all | solution.py:112
Sparse Core Ops, SparseCore 0:
  11.1 125.4 all-gather.2
  193.8 96.8 all-gather.4
where the time goes:
time: 318 us; the launch traced here: 317 us
  waiting for transfers between devices  200 us (63%)
  matrix products  36.8 us (12%)
  starting transfers between devices  33.7 us (11%)
  local copies, waits for them, and re-layouts  19.8 us (6%)
  between operations  14.3 us (4%)
  other arithmetic  12.6 us (4%)
    all_gather x1, waiting for transfers between devices, on_device(): whole_weights = lax.all_gather(flat_weights, 'dp', axis=0, tiled=True)  75.9 us
    all_to_all x1, waiting for transfers between devices, on_device(): lax.all_to_all(parts.reshape(local_rows, mp_devices, -1), 'mp', split_axi...  42.3 us
    all_to_all x1, waiting for transfers between devices, on_device(): lax.all_to_all(tokens, 'dp', split_axis=1, concat_axis=0, tiled=True)  33.3 us
    all_gather x1, waiting for transfers between devices, on_device(): gathered = lax.all_gather(dqkv, 'dp', axis=0, tiled=True)  31.4 us
    ppermute x8, starting transfers between devices, shifted(): return lax.ppermute(block, axis, route)  18 us
    ppermute x8, waiting for transfers between devices, shifted(): return lax.ppermute(block, axis, route)  16.8 us
    unnamed x21, local copies, waits for them, and re-layouts  11.2 us
    dot_general x1, matrix products, on_device(): lax.dot_general(columns, split_by_modality_major(gathered, token_image),...  9.91 us
  transfers between devices with their start and end apart: 12, of which 7 were waited for; matrix products, arithmetic and copies ran while one was open for 9% of the time, Pallas kernels for 0%

commit v1 on v0

--- a/solution.py
+++ b/solution.py
@@ -43,7 +43,15 @@
     token_image = jnp.repeat(block_modality, BLOCK) == 1
     my_image = lax.dynamic_slice_in_dim(token_image, my_index * local_rows, local_rows, 0)
     flat_weights = weights.reshape(width_rows, 2, 3 * head_width)
-    whole_weights = lax.all_gather(flat_weights, "dp", axis=0, tiled=True)
+    whole_weights = jnp.concatenate(
+        jax.lax.all_to_all(
+            jnp.stack([flat_weights for _ in range(jax.lax.axis_size("dp"))], 0),
+            "dp",
+            split_axis=0,
+            concat_axis=0,
+        ),
+        axis=0,
+    )
     columns = lax.all_to_all(tokens, "dp", split_axis=1, concat_axis=0, tiled=True)
     whole_weights, columns = lax.optimization_barrier((whole_weights, columns))
     stacked_weights = whole_weights.reshape(-1, 3 * head_width)

time: 318 us -> 460 us (1.45)
  waiting for transfers between devices: 200 us -> 312 us
  local copies, waits for them, and re-layouts: 19.8 us -> 39.1 us
  starting transfers between devices: 33.7 us -> 44.6 us
    all_to_all x0 -> x1, waiting for transfers between devices: none -> 194 us  [on_device(): jax.lax.all_to_all(jnp.stack([flat_weights for _ in range(jax.lax.axis_si...]
    all_gather x1 -> x0, waiting for transfers between devices: 75.9 us -> none  [on_device(): whole_weights = lax.all_gather(flat_weights, 'dp', axis=0, tiled=True)]
    reshape x0 -> x1, local copies, waits for them, and re-layouts: none -> 11.4 us  [on_device(): jnp.concatenate(jax.lax.all_to_all(jnp.stack([flat_weights for _ in range...]
    all_to_all x1, waiting for transfers between devices: 33.3 us -> 26.2 us  [on_device(): lax.all_to_all(tokens, 'dp', split_axis=1, concat_axis=0, tiled=True)]
    ppermute x8, waiting for transfers between devices: 16.8 us -> 10.2 us  [shifted(): return lax.ppermute(block, axis, route)]
    another operation x0 -> x1, local copies, waits for them, and re-layouts: none -> 5.96 us  [on_device(): jnp.stack([flat_weights for _ in range(jax.lax.axis_size('dp'))], 0)]
    all_to_all x0 -> x1, starting transfers between devices: none -> 5.8 us  [on_device(): jax.lax.all_to_all(jnp.stack([flat_weights for _ in range(jax.lax.axis_si...]
    all_gather x1, waiting for transfers between devices: 31.4 us -> 37.1 us  [on_device(): gathered = lax.all_gather(dqkv, 'dp', axis=0, tiled=True)]
  transfers between devices with their start and end apart: 12 -> 12, of which waited for: 7 -> 7; matrix products, arithmetic and copies ran while one was open for 9% -> 6% of each run, Pallas kernels for 0% -> 0%
where the time goes in v1:
time: 460 us; the launch traced here: 458 us
  waiting for transfers between devices  312 us (68%)
  starting transfers between devices  44.6 us (10%)
  local copies, waits for them, and re-layouts  39.1 us (8%)
  matrix products  36 us (8%)
  between operations  14.3 us (3%)
  other arithmetic  12.7 us (3%)
    all_to_all x1, waiting for transfers between devices, on_device(): jax.lax.all_to_all(jnp.stack([flat_weights for _ in range(jax.lax.axis_si...  194 us
    all_to_all x1, waiting for transfers between devices, on_device(): lax.all_to_all(parts.reshape(local_rows, mp_devices, -1), 'mp', split_axi...  44.7 us
    all_gather x1, waiting for transfers between devices, on_device(): gathered = lax.all_gather(dqkv, 'dp', axis=0, tiled=True)  37.1 us
    all_to_all x1, waiting for transfers between devices, on_device(): lax.all_to_all(tokens, 'dp', split_axis=1, concat_axis=0, tiled=True)  26.2 us
    ppermute x8, starting transfers between devices, shifted(): return lax.ppermute(block, axis, route)  23 us
    unnamed x25, local copies, waits for them, and re-layouts  13.3 us
    reshape x1, local copies, waits for them, and re-layouts, on_device(): jnp.concatenate(jax.lax.all_to_all(jnp.stack([flat_weights for _ in range...  11.4 us
    ppermute x8, waiting for transfers between devices, shifted(): return lax.ppermute(block, axis, route)  10.2 us
  transfers between devices with their start and end apart: 12, of which 7 were waited for; matrix products, arithmetic and copies ran while one was open for 6% of the time, Pallas kernels for 0%

profile of v1, /device:TPU:33, one launch (start us, length us, event | category | flops | bytes accessed | tf_op | source)
XLA Modules:
  0.0 458.5 jit_solution(4023950677850059465)
XLA Ops:
  7.2 4.1 copy.48
  11.3 7.6 %all-to-all-start.1 = ((bf16[256,16,256]{0,2,1:T(8,128)(2,1)}), bf16[256,16,256]{0,2,1:T(8,128)(2,1)S(1)}, u32[]{:S(2)}, u32[]{:S(2)}) async-start(bf16[256,16,256]{0,2,1:T(8,128)(2,1)} %bitcast.81), calls=%async_computation.1 | async-start | bytes 4194304 | tf_op jit(solution)/shard_map/all_to_all | solution.py:55
  18.9 2.2 copy.46
  21.1 26.2 %all-to-all-done.1 = bf16[256,16,256]{0,2,1:T(8,128)(2,1)S(1)} async-done(((bf16[256,16,256]{0,2,1:T(8,128)(2,1)}), bf16[256,16,256]{0,2,1:T(8,128)(2,1)S(1)}, u32[]{:S(2)}, u32[]{:S(2)}) %all-to-all-start.1) | async-done | bytes 2097184 | tf_op jit(solution)/shard_map/all_to_all | solution.py:55
  48.6 6.0 %stack.24 = bf16[16,256,2,768]{1,3,2,0:T(8,128)(2,1)} broadcast(bf16[256,2,768]{0,2,1:T(8,128)(2,1)S(1)} %bitcast.83), dimensions={1,2,3} | broadcast | bytes 13369344 | tf_op jit(solution)/shard_map/stack | solution.py:48
  54.6 5.8 %all-to-all-start = ((bf16[16,256,2,768]{1,3,2,0:T(8,128)(2,1)}), bf16[16,256,2,768]{1,3,2,0:T(8,128)(2,1)}, u32[]{:S(2)}, u32[]{:S(2)}) async-start(bf16[16,256,2,768]{1,3,2,0:T(8,128)(2,1)} %stack.24), calls=%async_computation | async-start | bytes 25165824 | tf_op jit(solution)/shard_map/all_to_all | solution.py:47
  60.8 2.4 select_bitcast_fusion.1
  63.2 3.9 copy.49
  67.1 193.6 %all-to-all-done = bf16[16,256,2,768]{1,3,2,0:T(8,128)(2,1)} async-done(((bf16[16,256,2,768]{1,3,2,0:T(8,128)(2,1)}), bf16[16,256,2,768]{1,3,2,0:T(8,128)(2,1)}, u32[]{:S(2)}, u32[]{:S(2)}) %all-to-all-start) | async-done | bytes 12582944 | tf_op jit(solution)/shard_map/all_to_all | solution.py:47
  260.7 11.4 %copy.72 = bf16[16,2,96,8,256]{4,3,0,2,1:T(8,128)(2,1)} copy(bf16[16,2,96,8,256]{4,3,2,1,0:T(8,128)(2,1)} %bitcast.30) | data formatting | bytes 25165824 | tf_op jit(solution)/shard_map/reshape | solution.py:46
  272.1 8.0 %fusion.22 = bf16[256,768]{1,0:T(8,128)(2,1)S(1)} fusion(bf16[4096,2,768]{0,2,1:T(8,128)(2,1)} %bitcast.76, bf16[256,4096,1]{1,0,2:T(8,128)(2,1)S(1)} %copy-done.4, bf16[256,4096,1]{1,0,2:T(8,128)(2,1)S(1)} %copy-done.3), kind=kOutput, calls=%fused_computation.35 | convolution fusion | flops 3223519232 | bytes 17170432 | tf_op jit(solution)/shard_map/dot_general | solution.py:58
  283.1 9.9 %collective-permute-start.2 = (bf16[256,2,2,128]{3,0,2,1:T(8,128)(2,1)S(1)}, bf16[256,2,2,128]{3,0,2,1:T(8,128)(2,1)S(1)}, u32[]{:S(2)}, u32[]{:S(2)}) collective-permute-start(bf16[256,2,2,128]{3,0,2,1:T(8,128)(2,1)S(1)} %copy.68), channel_id=1, source_target_pairs={{0,32},{16,48},{32,64},{48,80},{64,96},{80,112},{96,128},{112,144}... | collective-permute-start | bytes 786440 | tf_op jit(solution)/shard_map/ppermute | solution.py:14
  293.4 4.5 collective-permute-start.3
  302.8 2.5 fusion.45
  305.3 2.2 multiply_reduce_fusion
  313.0 2.1 collective-permute-start.4
  316.8 8.5 %collective-permute-done.6 = bf16[256,2,2,128]{0,3,2,1:T(8,128)(2,1)S(1)} collective-permute-done((bf16[256,2,2,128]{0,3,2,1:T(8,128)(2,1)S(1)}, bf16[256,2,2,128]{0,3,2,1:T(8,128)(2,1)S(1)}, u32[]{:S(2)}, u32[]{:S(2)}) %collective-permute-start.6) | collective-permute-done | bytes 262176 | tf_op jit(solution)/shard_map/ppermute | solution.py:14
  328.0 8.3 %convolution_convert_fusion = bf16[256,4096]{1,0:T(8,128)(2,1)S(1)} fusion(bf16[4096,1536]{0,1:T(8,128)(2,1)} %bitcast.77, bf16[256,768]{0,1:T(8,128)(2,1)S(1)} %get-tuple-element.28, bf16[256,768]{0,1:T(8,128)(2,1)S(1)} %get-tuple-element.27), kind=kOutput, calls=%fused_computation.7 | convolution fusion | flops 3223846912 | bytes 15466496 | tf_op jit(solution)/shard_map/dot_general | solution.py:114
  337.9 8.1 %all-to-all-start.2 = ((bf16[256,16,256]{2,0,1:T(8,128)(2,1)}), bf16[256,16,256]{2,0,1:T(8,128)(2,1)S(1)}, u32[]{:S(2)}, u32[]{:S(2)}) async-start(bf16[256,16,256]{2,0,1:T(8,128)(2,1)} %bitcast.80), calls=%async_computation.2 | async-start | bytes 4194304 | tf_op jit(solution)/shard_map/all_to_all | solution.py:120
  346.1 2.6 convolution_convert_fusion.1
  349.4 44.7 %all-to-all-done.2 = bf16[256,16,256]{2,0,1:T(8,128)(2,1)S(1)} async-done(((bf16[256,16,256]{2,0,1:T(8,128)(2,1)}), bf16[256,16,256]{2,0,1:T(8,128)(2,1)S(1)}, u32[]{:S(2)}, u32[]{:S(2)}) %all-to-all-start.2) | async-done | bytes 2097184 | tf_op jit(solution)/shard_map/all_to_all | solution.py:120
  395.1 37.1 %all-gather.2.cloned.1.call-done = bf16[4096,768]{0,1:T(8,128)(2,1)} async-done(((bf16[256,768]{0,1:T(8,128)(2,1)}), bf16[4096,768]{0,1:T(8,128)(2,1)}) %all-gather.2.cloned.1.call-update) | async-done | bytes 6291472 | tf_op jit(solution)/shard_map/all_gather | solution.py:124
  432.2 6.3 %broadcast_select_fusion.1 = (bf16[4096,768]{0,1:T(8,128)(2,1)S(1)}, bf16[4096,768]{0,1:T(8,128)(2,1)}) fusion(bf16[4096,768]{0,1:T(8,128)(2,1)} %all-gather.2.cloned.1.call-done, pred[4096]{0:T(1024)(128)(4,1)S(1)} %broadcast_bitcast_fusion), kind=kLoop, calls=%fused_computation.6 | loop fusion | flops 6291456 | bytes 18878464 | tf_op jit(solution)/shard_map/jit(_where)/select_n | solution.py:26
  438.5 9.9 %fusion.15 = bf16[256,1536]{1,0:T(8,128)(2,1)} fusion(bf16[4096,256]{1,0:T(8,128)(2,1)} %bitcast.85, bf16[4096,768]{0,1:T(8,128)(2,1)} %get-tuple-element.20, bf16[4096,768]{0,1:T(8,128)(2,1)S(1)} %get-tuple-element.19), kind=kOutput, calls=%fused_computation.27 | convolution fusion | flops 3246784512 | bytes 15466496 | tf_op jit(solution)/shard_map/dot_general | solution.py:125
  (60 shorter events, 26.2 us)
Async XLA Ops:
  11.3 36.1 %all-to-all-start.1 = ((bf16[256,16,256]{0,2,1:T(8,128)(2,1)}), bf16[256,16,256]{0,2,1:T(8,128)(2,1)S(1)}, u32[]{:S(2)}, u32[]{:S(2)}) async-start(bf16[256,16,256]{0,2,1:T(8,128)(2,1)} %bitcast.81), calls=%async_computation.1 | async-start | bytes 4194304 | tf_op jit(solution)/shard_map/all_to_all | solution.py:55
  47.3 1.3 copy-start.1
  54.6 5.9 %copy-start.7 = (s32[32]{0:T(128)S(1)}, s32[32]{0:T(128)}, u32[]{:S(2)}) copy-start(s32[32]{0:T(128)} %param.7) | copy-start | bytes 388
  54.6 6.0 %copy-start.6 = (s32[4096]{0:T(1024)S(1)}, s32[4096]{0:T(1024)}, u32[]{:S(2)}) copy-start(s32[4096]{0:T(1024)} %param.8) | copy-start | bytes 49156
  54.6 6.2 %copy-start = (bf16[256,4096]{1,0:T(8,128)(2,1)S(1)}, bf16[256,4096]{1,0:T(8,128)(2,1)}, u32[]{:S(2)}) copy-start(bf16[256,4096]{1,0:T(8,128)(2,1)} %param.5) | copy-start | bytes 6291460
  54.6 206.1 %all-to-all-start = ((bf16[16,256,2,768]{1,3,2,0:T(8,128)(2,1)}), bf16[16,256,2,768]{1,3,2,0:T(8,128)(2,1)}, u32[]{:S(2)}, u32[]{:S(2)}) async-start(bf16[16,256,2,768]{1,3,2,0:T(8,128)(2,1)} %stack.24), calls=%async_computation | async-start | bytes 25165824 | tf_op jit(solution)/shard_map/all_to_all | solution.py:47
  60.4 371.8 %all-gather.2.cloned.1.call-start = ((), (), s32[]{:S(2)}) async-start(), calls=%async_computation.3 | async-start | bytes 6684672 | tf_op jit(solution)/shard_map/all_gather | solution.py:124
  260.7 11.4 %copy-start.3 = (bf16[256,4096,1]{1,0,2:T(8,128)(2,1)S(1)}, bf16[256,4096,1]{1,0,2:T(8,128)(2,1)}, u32[]{:S(2)}) copy-start(bf16[256,4096,1]{1,0,2:T(8,128)(2,1)} %get-tuple-element.21) | copy-start | bytes 6291460
  260.7 11.4 %copy-start.4 = (bf16[256,4096,1]{1,0,2:T(8,128)(2,1)S(1)}, bf16[256,4096,1]{1,0,2:T(8,128)(2,1)}, u32[]{:S(2)}) copy-start(bf16[256,4096,1]{1,0,2:T(8,128)(2,1)} %get-tuple-element.22) | copy-start | bytes 6291460
  280.1 13.2 %copy-start.5 = (bf16[256,256]{1,0:T(8,128)(2,1)S(1)}, bf16[256,256]{1,0:T(8,128)(2,1)}, u32[]{:S(2)}) copy-start(bf16[256,256]{1,0:T(8,128)(2,1)} %param.9) | copy-start | bytes 393220
  280.5 17.6 %collective-permute-start = (bf16[256,2,2,128]{3,0,2,1:T(8,128)(2,1)S(1)}, bf16[256,2,2,128]{3,0,2,1:T(8,128)(2,1)S(1)}, u32[]{:S(2)}, u32[]{:S(2)}) collective-permute-start(bf16[256,2,2,128]{3,0,2,1:T(8,128)(2,1)S(1)} %copy.68), channel_id=1, source_target_pairs={{0,64},{16,80},{32,96},{48,112},{64,128},{80,144},{96,160},{112,17... | collective-permute-start | bytes 786440 | tf_op jit(solution)/shard_map/ppermute | solution.py:14
  281.8 17.0 %collective-permute-start.1 = (bf16[256,2,2,128]{3,0,2,1:T(8,128)(2,1)S(1)}, bf16[256,2,2,128]{3,0,2,1:T(8,128)(2,1)S(1)}, u32[]{:S(2)}, u32[]{:S(2)}) collective-permute-start(bf16[256,2,2,128]{3,0,2,1:T(8,128)(2,1)S(1)} %copy.68), channel_id=1, source_target_pairs={{0,48},{16,64},{32,80},{48,96},{64,112},{80,128},{96,144},{112,160... | collective-permute-start | bytes 786440 | tf_op jit(solution)/shard_map/ppermute | solution.py:14
  283.1 16.5 %collective-permute-start.2 = (bf16[256,2,2,128]{3,0,2,1:T(8,128)(2,1)S(1)}, bf16[256,2,2,128]{3,0,2,1:T(8,128)(2,1)S(1)}, u32[]{:S(2)}, u32[]{:S(2)}) collective-permute-start(bf16[256,2,2,128]{3,0,2,1:T(8,128)(2,1)S(1)} %copy.68), channel_id=1, source_target_pairs={{0,32},{16,48},{32,64},{48,80},{64,96},{80,112},{96,128},{112,144}... | collective-permute-start | bytes 786440 | tf_op jit(solution)/shard_map/ppermute | solution.py:14
  293.4 7.8 %collective-permute-start.3 = (bf16[256,2,2,128]{3,0,2,1:T(8,128)(2,1)S(1)}, bf16[256,2,2,128]{3,0,2,1:T(8,128)(2,1)S(1)}, u32[]{:S(2)}, u32[]{:S(2)}) collective-permute-start(bf16[256,2,2,128]{3,0,2,1:T(8,128)(2,1)S(1)} %copy.68), channel_id=1, source_target_pairs={{0,16},{16,32},{32,48},{48,64},{64,80},{80,96},{96,112},{112,128},... | collective-permute-start | bytes 786440 | tf_op jit(solution)/shard_map/ppermute | solution.py:14
  305.3 2.6 copy-start.2
  309.1 7.7 %collective-permute-start.7 = (bf16[256,2,2,128]{0,3,2,1:T(8,128)(2,1)S(1)}, bf16[256,2,2,128]{0,3,2,1:T(8,128)(2,1)S(1)}, u32[]{:S(2)}, u32[]{:S(2)}) collective-permute-start(bf16[256,2,2,128]{0,3,2,1:T(8,128)(2,1)S(1)} %get-tuple-element.24), channel_id=1, source_target_pairs={{64,0},{80,16},{96,32},{112,48},{128,64},{144,80},{160,96},{176,11... | collective-permute-start | bytes 786440 | tf_op jit(solution)/shard_map/ppermute | solution.py:14
  310.4 14.9 %collective-permute-start.6 = (bf16[256,2,2,128]{0,3,2,1:T(8,128)(2,1)S(1)}, bf16[256,2,2,128]{0,3,2,1:T(8,128)(2,1)S(1)}, u32[]{:S(2)}, u32[]{:S(2)}) collective-permute-start(bf16[256,2,2,128]{0,3,2,1:T(8,128)(2,1)S(1)} %get-tuple-element.25), channel_id=1, source_target_pairs={{48,0},{64,16},{80,32},{96,48},{112,64},{128,80},{144,96},{160,112... | collective-permute-start | bytes 786440 | tf_op jit(solution)/shard_map/ppermute | solution.py:14
  311.7 13.6 %collective-permute-start.5 = (bf16[256,2,2,128]{0,3,2,1:T(8,128)(2,1)S(1)}, bf16[256,2,2,128]{0,3,2,1:T(8,128)(2,1)S(1)}, u32[]{:S(2)}, u32[]{:S(2)}) collective-permute-start(bf16[256,2,2,128]{0,3,2,1:T(8,128)(2,1)S(1)} %get-tuple-element.26), channel_id=1, source_target_pairs={{32,0},{48,16},{64,32},{80,48},{96,64},{112,80},{128,96},{144,112}... | collective-permute-start | bytes 786440 | tf_op jit(solution)/shard_map/ppermute | solution.py:14
  313.0 13.0 %collective-permute-start.4 = (bf16[256,2,2,128]{0,3,2,1:T(8,128)(2,1)S(1)}, bf16[256,2,2,128]{0,3,2,1:T(8,128)(2,1)S(1)}, u32[]{:S(2)}, u32[]{:S(2)}) collective-permute-start(bf16[256,2,2,128]{0,3,2,1:T(8,128)(2,1)S(1)} %get-tuple-element.23), channel_id=1, source_target_pairs={{16,0},{32,16},{48,32},{64,48},{80,64},{96,80},{112,96},{128,112},... | collective-permute-start | bytes 786440 | tf_op jit(solution)/shard_map/ppermute | solution.py:14
  337.9 56.2 %all-to-all-start.2 = ((bf16[256,16,256]{2,0,1:T(8,128)(2,1)}), bf16[256,16,256]{2,0,1:T(8,128)(2,1)S(1)}, u32[]{:S(2)}, u32[]{:S(2)}) async-start(bf16[256,16,256]{2,0,1:T(8,128)(2,1)} %bitcast.80), calls=%async_computation.2 | async-start | bytes 4194304 | tf_op jit(solution)/shard_map/all_to_all | solution.py:120
Sparse Core Ops, SparseCore 0:
  327.1 105.0 all-gather.1
